TPU v7x, 256 devices: a whole 4x4x8 slice. The times are simulated.
256 devices in a mesh: blk: 32 (over x, y, core), sub: 8 (over z).
Axes of the slice: x: 4, y: 4, z: 8, core: 2. Of those that a mesh axis runs over, the one named last changes fastest.
Arguments:
- block_vec: bfloat16 [64, 512, 512], P('blk', 'sub'), may hold values from -6 to 6
- left_factor: bfloat16 [8, 512, 512], replicated, may hold values from -0.25 to 0.25
- right_factor: bfloat16 [8, 512, 512], replicated, may hold values from -0.25 to 0.25
- pairs: int32 [32, 32, 2, 3], replicated, may hold values from 0 to 7, as said below
- pair_count: int32 [32, 32], replicated, may hold values from 1 to 2, as said below
- left_basis: bfloat16 [64, 512, 512], P('blk'), may hold values from -0.25 to 0.25
- left_dual: bfloat16 [64, 512, 512], P('blk'), may hold values from -0.25 to 0.25
- right_eigenvector_matrix: bfloat16 [64, 512, 512], P('blk'), may hold values from -0.25 to 0.25
- right_dual: bfloat16 [64, 512, 512], P('blk'), may hold values from -0.25 to 0.25
- left_rates: float32 [64, 512], P('blk', 'sub'), may hold values from 0.5 to 8
- right_rates: float32 [64, 512], P('blk'), may hold values from 0.5 to 8
Outputs:
- next_vec: float32 [64, 512, 512], P('blk', None, 'sub')
Inputs may be any that keep to these rules, and one draw needn't show every extreme that they name: `pairs`: entry [g, h, c, 0] is a source block index within group g, [g, h, c, 1] a target block index within group h (0 to 1), and [g, h, c, 2] a term index (0 to 7); where g equals h, source and target differ. For some target group h, pair_count[g, h] is 2 for every g.
All inputs are finite; a program needn't handle non-finite values.
Results may differ from a plain program's by a relative error of at most 0.023.
Values may be sent and summed in bfloat16 or wider, within the bound.
No kernel may reach another device: no remote copies, remote signals or barrier semaphores. Data moves between devices by JAX's collectives and lax.ppermute only.
A program may use at most 64 MiB of HBM per device.

v0:
```python
import jax
import jax.numpy as jnp
from jax import lax
from jax.sharding import PartitionSpec as P


def local(
    block_vec,
    left_factor,
    right_factor,
    pairs,
    pair_count,
    left_basis,
    left_dual,
    right_eigenvector_matrix,
    right_dual,
    left_rates,
    right_rates,
):
    owner = lax.axis_index("blk")
    groups = lax.axis_size("blk")
    local_blocks = block_vec.shape[0]
    row_count = block_vec.shape[1]
    width_two = block_vec.shape[2]
    slots_per = pairs.shape[2]
    term_total = left_factor.shape[0]
    all_count = groups * local_blocks
    incoming = lax.dynamic_index_in_dim(pairs, owner, 1, keepdims=False)
    counts = lax.dynamic_index_in_dim(pair_count, owner, 1, keepdims=False)
    live_mask = (jnp.arange(slots_per)[None, :] < counts[:, None]).astype(jnp.float32)
    target_term = incoming[..., 1] * term_total + incoming[..., 2]
    source = jnp.arange(groups, dtype=jnp.int32)[:, None] * local_blocks + incoming[..., 0]
    key_onehot = (
        target_term[..., None] == jnp.arange(local_blocks * term_total)[None, None, :]
    ).astype(jnp.float32) * live_mask[..., None]
    source_onehot = (source[..., None] == jnp.arange(all_count)[None, None, :]).astype(jnp.float32)
    weights = jnp.einsum("gqk,gqs->ks", key_onehot, source_onehot).astype(jnp.bfloat16)
    everything = lax.all_gather(block_vec, "blk", axis=0, tiled=True)
    pooled = jnp.einsum(
        "ks,srn->krn", weights, everything, preferred_element_type=jnp.float32
    ).astype(jnp.bfloat16)
    pooled = pooled.reshape(local_blocks, term_total, row_count, width_two)
    right_done = jnp.einsum(
        "ktrn,tmn->ktrm", pooled, right_factor, preferred_element_type=jnp.float32
    ).astype(jnp.bfloat16)
    right_cols = lax.all_to_all(right_done, "sub", split_axis=3, concat_axis=2, tiled=True)
    summed = jnp.einsum(
        "tab,ktbc->kac", left_factor, right_cols, preferred_element_type=jnp.float32
    ).astype(jnp.bfloat16)
    dual_cols = jnp.einsum(
        "jab,jbc->jac", left_dual, summed, preferred_element_type=jnp.float32
    ).astype(jnp.bfloat16)
    dual_rows = lax.all_to_all(dual_cols, "sub", split_axis=1, concat_axis=2, tiled=True)
    mixed = jnp.einsum("jrn,jmn->jrm", dual_rows, right_dual, preferred_element_type=jnp.float32)
    scaled = (mixed / (left_rates[:, :, None] + right_rates[:, None, :])).astype(jnp.bfloat16)
    basis_rows = jnp.einsum(
        "jrm,jkm->jrk", scaled, right_eigenvector_matrix, preferred_element_type=jnp.float32
    ).astype(jnp.bfloat16)
    basis_cols = lax.all_to_all(basis_rows, "sub", split_axis=2, concat_axis=1, tiled=True)
    return jnp.einsum("jab,jbc->jac", left_basis, basis_cols, preferred_element_type=jnp.float32)


def solution(mesh):
    placed = (
        P("blk", "sub", None),
        P(),
        P(),
        P(),
        P(),
        P("blk", None, None),
        P("blk", None, None),
        P("blk", None, None),
        P("blk", None, None),
        P("blk", "sub"),
        P("blk", None),
    )
    return jax.shard_map(
        local, mesh=mesh, in_specs=placed, out_specs=P("blk", None, "sub"), check_vma=False
    )
```

profile of v0, /device:TPU:2, one launch (start us, length us, event | category | flops | bytes accessed | tf_op | source)
XLA Modules:
  0.0 167.2 jit_solution(14784271772205998171)
XLA Ops:
  6.5 0.7 all-gather.2.cloned.1.call-update
  7.3 1.1 constant_dynamic-slice_fusion
  8.4 0.9 dynamic-slice_reduce_fusion
  9.4 54.3 %all-gather.2.cloned.1.call-done = bf16[64,64,512]{2,1,0:T(8,128)(2,1)} async-done(((bf16[2,64,512]{2,1,0:T(8,128)(2,1)}), bf16[64,64,512]{2,1,0:T(8,128)(2,1)}) %all-gather.2.cloned.1.call-update) | async-done | bytes 4194320 | tf_op jit(solution)/shard_map/all_gather | solution.py:38
  63.7 6.7 %fusion.15 = bf16[2,8,64,512]{3,1,0,2:T(8,128)(2,1)S(1)} fusion(bf16[64,64,512]{2,1,0:T(8,128)(2,1)} %all-gather.2.cloned.1.call-done, s32[32,2]{0,1:T(2,128)S(1)} %get-tuple-element.6, bf16[32,2]{0,1:T(2,128)(2,1)S(1)} %compare_convert_fusion, s32[32,2]{0,1:T(2,128)S(1)} %get-tuple-element.5), kind=kOutput, calls=%fused_computation.10 | convolution fusion | flops 67770368 | bytes 5243520 | tf_op jit(solution)/shard_map/ks,srn->krn/dot_general | solution.py:39
  70.4 4.8 %fusion.12 = bf16[2,8,64,512]{3,2,0,1:T(8,128)(2,1)} fusion(bf16[8,512,512]{2,1,0:T(8,128)(2,1)} %param.13, bf16[2,8,64,512]{3,1,0,2:T(8,128)(2,1)S(1)} %fusion.15), kind=kOutput, calls=%fused_computation.9 | convolution fusion | flops 537395200 | bytes 6291456 | tf_op jit(solution)/shard_map/ktrn,tmn->ktrm/dot_general | solution.py:43
  75.2 4.7 %copy.28 = bf16[2,8,64,512]{2,0,1,3:T(2,128)(2,1)S(1)} copy(bf16[2,8,64,512]{3,2,0,1:T(8,128)(2,1)} %fusion.12) | data formatting | bytes 2097152 | tf_op jit(solution)/shard_map/convert_element_type | solution.py:45
  80.0 2.7 %reshape.46 = bf16[8,2,32768]{2,1,0:T(2,128)(2,1)} reshape(bf16[512,8,2,64]{3,2,1,0:T(2,128)(2,1)S(1)} %bitcast.85) | data formatting | bytes 2097152
  82.6 36.3 %all_to_all.54 = bf16[8,2,32768]{2,1,0:T(2,128)(2,1)} all-to-all(bf16[8,2,32768]{2,1,0:T(2,128)(2,1)} %reshape.46), channel_id=1, replica_groups=mesh['blk'=32,'sub'=8] {'sub'}, dimensions={0} | all-to-all | bytes 2097152 | tf_op jit(solution)/shard_map/all_to_all | solution.py:46
  118.9 3.1 %reshape.47 = bf16[512,8,2,64]{3,2,1,0:T(2,128)(2,1)S(1)} reshape(bf16[8,2,32768]{2,1,0:T(2,128)(2,1)} %all_to_all.54) | data formatting | bytes 2097152
  122.0 2.7 %copy.47 = bf16[2,8,64,8,64]{2,3,4,1,0:T(8,128)(2,1)} copy(bf16[2,8,64,8,64]{2,0,1,4,3:T(2,128)(2,1)S(1)} %bitcast.86) | data formatting | bytes 2097152 | tf_op jit(solution)/shard_map/all_to_all | solution.py:46
  124.7 3.2 %all_to_all.42 = bf16[2,8,512,64]{2,3,1,0:T(8,128)(2,1)S(1)} reshape(bf16[2,8,8,64,64]{3,2,4,1,0:T(8,128)(2,1)} %bitcast.87) | data formatting | bytes 2097152 | tf_op jit(solution)/shard_map/all_to_all | solution.py:46
  127.9 4.0 %fusion.25 = bf16[2,512,64]{1,2,0:T(8,128)(2,1)S(1)} fusion(bf16[2,512,512]{2,1,0:T(8,128)(2,1)S(1)} %copy-done, bf16[2,8,512,64]{2,3,1,0:T(8,128)(2,1)S(1)} %all_to_all.42, bf16[8,512,512]{2,1,0:T(8,128)(2,1)} %param.12), kind=kOutput, calls=%fused_computation.18 | convolution fusion | flops 604110848 | bytes 6422528 | tf_op jit(solution)/shard_map/jab,jbc->jac/dot_general | solution.py:50
  132.1 0.2 reshape.48
  132.3 11.5 %all_to_all.55 = bf16[8,2,4096]{2,1,0:T(2,128)(2,1)S(1)} all-to-all(bf16[8,2,4096]{2,1,0:T(2,128)(2,1)S(1)} %reshape.48), channel_id=1, replica_groups=mesh['blk'=32,'sub'=8] {'sub'}, dimensions={0} | all-to-all | bytes 262144 | tf_op jit(solution)/shard_map/all_to_all | solution.py:53
  143.8 0.2 reshape.49
  144.0 0.2 copy.49
  144.2 0.2 all_to_all.46
  144.4 2.3 %convolution_convert_fusion = bf16[2,64,512]{2,1,0:T(8,128)(2,1)S(1)} fusion(bf16[2,512,512]{2,1,0:T(8,128)(2,1)} %param.18, bf16[2,64,512]{2,1,0:T(8,128)(2,1)S(1)} %all_to_all.46, bf16[2,512,512]{2,1,0:T(8,128)(2,1)} %param.19, f32[2,512]{1,0:T(2,128)S(1)} %copy-done.2, f32[2,64]{1,0:T(2,128)S(1)} %copy-done.3), kind=kOutput, calls=%fused_computation.15 | convolution fusion | flops 134479872 | bytes 2363904 | tf_op jit(solution)/shard_map/jrm,jkm->jrk/dot_general | solution.py:56
  146.9 0.2 reshape.50
  147.1 11.5 %all_to_all.56 = bf16[8,2,4096]{2,1,0:T(2,128)(2,1)S(1)} all-to-all(bf16[8,2,4096]{2,1,0:T(2,128)(2,1)S(1)} %reshape.50), channel_id=1, replica_groups=mesh['blk'=32,'sub'=8] {'sub'}, dimensions={0} | all-to-all | bytes 262144 | tf_op jit(solution)/shard_map/all_to_all | solution.py:59
  158.6 0.2 reshape.51
  159.0 0.2 all_to_all.50
  159.2 1.1 convolution_bitcast_fusion
  (16 shorter events, 0.7 us)
Async XLA Ops:
  6.5 121.3 %copy-start = (bf16[2,512,512]{2,1,0:T(8,128)(2,1)S(1)}, bf16[2,512,512]{2,1,0:T(8,128)(2,1)}, u32[]{:S(2)}) copy-start(bf16[2,512,512]{2,1,0:T(8,128)(2,1)} %param.17) | copy-start | bytes 3145732
  6.5 57.1 %all-gather.2.cloned.1.call-start = ((), (), s32[]{:S(2)}) async-start(), calls=%async_computation.3 | async-start | bytes 4325376 | tf_op jit(solution)/shard_map/all_gather | solution.py:38
  127.9 16.5 %copy-start.2 = (f32[2,512]{1,0:T(2,128)S(1)}, f32[2,512]{1,0:T(2,128)}, u32[]{:S(2)}) copy-start(f32[2,512]{1,0:T(2,128)} %param.21) | copy-start | bytes 12292
  127.9 16.5 %copy-start.3 = (f32[2,64]{1,0:T(2,128)S(1)}, f32[2,64]{1,0:T(2,128)}, u32[]{:S(2)}) copy-start(f32[2,64]{1,0:T(2,128)} %param.20) | copy-start | bytes 1540
  131.9 27.3 %copy-start.1 = (bf16[2,512,512]{2,1,0:T(8,128)(2,1)S(1)}, bf16[2,512,512]{2,1,0:T(8,128)(2,1)}, u32[]{:S(2)}) copy-start(bf16[2,512,512]{2,1,0:T(8,128)(2,1)} %param.16) | copy-start | bytes 3145732
Sparse Core Ops, SparseCore 0:
  9.9 53.7 all-gather.1
where the time goes:
time: 168 us; the launch traced here: 167 us
  blocking collectives  59.2 us (35%)
  waiting for transfers between devices  55 us (33%)
  local copies, waits for them, and re-layouts  20.5 us (12%)
  matrix products  19 us (11%)
  between operations  13.6 us (8%)
    all_gather x1, waiting for transfers between devices, local(): everything = lax.all_gather(block_vec, 'blk', axis=0, tiled=True)  54.3 us
    all_to_all x1, blocking collectives, local(): lax.all_to_all(right_done, 'sub', split_axis=3, concat_axis=2, tiled=True)  36.3 us
    all_to_all x1, blocking collectives, local(): lax.all_to_all(dual_cols, 'sub', split_axis=1, concat_axis=2, tiled=True)  11.5 us
    all_to_all x1, blocking collectives, local(): lax.all_to_all(basis_rows, 'sub', split_axis=2, concat_axis=1, tiled=True)  11.5 us
    dot_general x1, matrix products, local(): jnp.einsum('ks,srn->krn', weights, everything, preferred_element_type=jnp...  6.75 us
    unnamed x14, local copies, waits for them, and re-layouts  6.67 us
    all_to_all x2, local copies, waits for them, and re-layouts, local(): lax.all_to_all(right_done, 'sub', split_axis=3, concat_axis=2, tiled=True)  5.88 us
    dot_general x1, matrix products, local(): jnp.einsum('ktrn,tmn->ktrm', pooled, right_factor, preferred_element_type...  4.8 us
  transfers between devices with their start and end apart: 1, of which 1 were waited for; matrix products, arithmetic and copies ran while one was open for 1% of the time, Pallas kernels for 0%

commit v1 on v0

--- a/solution.py
+++ b/solution.py
@@ -43,7 +43,10 @@
     right_done = jnp.einsum(
         "ktrn,tmn->ktrm", pooled, right_factor, preferred_element_type=jnp.float32
     ).astype(jnp.bfloat16)
-    right_cols = lax.all_to_all(right_done, "sub", split_axis=3, concat_axis=2, tiled=True)
+    right_cols = jnp.concatenate(
+        lax.all_to_all(jnp.stack(jnp.split(right_done, lax.axis_size("sub"), axis=3)), "sub", 0, 0),
+        axis=2,
+    )
     summed = jnp.einsum(
         "tab,ktbc->kac", left_factor, right_cols, preferred_element_type=jnp.float32
     ).astype(jnp.bfloat16)

time: 168 us -> 166 us (0.988)
    reshape x0 -> x3, local copies, waits for them, and re-layouts: none -> 6.82 us  [local(): jnp.concatenate(lax.all_to_all(jnp.stack(jnp.split(right_done, lax.axis_s...]
    all_to_all x2 -> x0, local copies, waits for them, and re-layouts: 5.88 us -> none  [local(): lax.all_to_all(right_done, 'sub', split_axis=3, concat_axis=2, tiled=True)]
    convert_element_type x1 -> x0, local copies, waits for them, and re-layouts: 4.74 us -> none  [local(): right_done = jnp.einsum('ktrn,tmn->ktrm', pooled, right_factor, preferred...]
    unnamed x14 -> x25, local copies, waits for them, and re-layouts: 6.67 us -> 9.54 us
where the time goes in v1:
time: 166 us; the launch traced here: 165 us
  blocking collectives  59 us (36%)
  waiting for transfers between devices  55 us (33%)
  local copies, waits for them, and re-layouts  19.7 us (12%)
  matrix products  18.1 us (11%)
  between operations  13.6 us (8%)
    all_gather x1, waiting for transfers between devices, local(): everything = lax.all_gather(block_vec, 'blk', axis=0, tiled=True)  54.3 us
    all_to_all x1, blocking collectives, local(): lax.all_to_all(jnp.stack(jnp.split(right_done, lax.axis_size('sub'), axis...  36.1 us
    all_to_all x1, blocking collectives, local(): lax.all_to_all(dual_cols, 'sub', split_axis=1, concat_axis=2, tiled=True)  11.5 us
    all_to_all x1, blocking collectives, local(): lax.all_to_all(basis_rows, 'sub', split_axis=2, concat_axis=1, tiled=True)  11.5 us
    unnamed x25, local copies, waits for them, and re-layouts  9.54 us
    reshape x3, local copies, waits for them, and re-layouts, local(): jnp.concatenate(lax.all_to_all(jnp.stack(jnp.split(right_done, lax.axis_s...  6.82 us
    dot_general x1, matrix products, local(): jnp.einsum('ks,srn->krn', weights, everything, preferred_element_type=jnp...  6.75 us
    dot_general x1, matrix products, local(): jnp.einsum('jab,jbc->jac', left_dual, summed, preferred_element_type=jnp....  4.3 us
  transfers between devices with their start and end apart: 1, of which 1 were waited for; matrix products, arithmetic and copies ran while one was open for 1% of the time, Pallas kernels for 0%

profile of v1, /device:TPU:2, one launch (start us, length us, event | category | flops | bytes accessed | tf_op | source)
XLA Modules:
  0.0 165.5 jit_solution(5505794938168404843)
XLA Ops:
  6.5 0.7 all-gather.2.cloned.1.call-update
  7.3 1.1 constant_dynamic-slice_fusion
  8.4 0.9 dynamic-slice_reduce_fusion
  9.4 54.3 %all-gather.2.cloned.1.call-done = bf16[64,64,512]{2,1,0:T(8,128)(2,1)} async-done(((bf16[2,64,512]{2,1,0:T(8,128)(2,1)}), bf16[64,64,512]{2,1,0:T(8,128)(2,1)}) %all-gather.2.cloned.1.call-update) | async-done | bytes 4194320 | tf_op jit(solution)/shard_map/all_gather | solution.py:38
  63.7 6.7 %fusion.15 = bf16[2,8,64,512]{3,1,0,2:T(8,128)(2,1)S(1)} fusion(bf16[64,64,512]{2,1,0:T(8,128)(2,1)} %all-gather.2.cloned.1.call-done, s32[32,2]{0,1:T(2,128)S(1)} %get-tuple-element.6, bf16[32,2]{0,1:T(2,128)(2,1)S(1)} %compare_convert_fusion, s32[32,2]{0,1:T(2,128)S(1)} %get-tuple-element.5), kind=kOutput, calls=%fused_computation.9 | convolution fusion | flops 67770368 | bytes 5243520 | tf_op jit(solution)/shard_map/ks,srn->krn/dot_general | solution.py:39
  70.4 3.8 %fusion.12 = bf16[2,8,64,512]{3,2,0,1:T(8,128)(2,1)S(1)} fusion(bf16[8,512,512]{2,1,0:T(8,128)(2,1)} %param.13, bf16[2,8,64,512]{3,1,0,2:T(8,128)(2,1)S(1)} %fusion.15), kind=kOutput, calls=%fused_computation.8 | convolution fusion | flops 537395200 | bytes 6291456 | tf_op jit(solution)/shard_map/ktrn,tmn->ktrm/dot_general | solution.py:43
  75.3 1.3 copy-done.1
  76.7 3.4 %reshape.54 = bf16[8,2,32768]{2,1,0:T(2,128)(2,1)S(1)} reshape(bf16[8,8,2,64,64]{4,3,2,1,0:T(8,128)(2,1)} %bitcast.116) | data formatting | bytes 2097152
  80.0 36.1 %all_to_all.41 = bf16[8,2,32768]{2,1,0:T(2,128)(2,1)} all-to-all(bf16[8,2,32768]{2,1,0:T(2,128)(2,1)S(1)} %reshape.54), channel_id=1, replica_groups=mesh['blk'=32,'sub'=8] {'sub'}, dimensions={0} | all-to-all | bytes 2097152 | tf_op jit(solution)/shard_map/all_to_all | solution.py:47
  116.1 3.1 %reshape.55 = bf16[8,8,2,64,64]{4,3,2,1,0:T(8,128)(2,1)S(1)} reshape(bf16[8,2,32768]{2,1,0:T(2,128)(2,1)} %all_to_all.41) | data formatting | bytes 2097152
  119.2 1.5 bitcast_bitcast_fusion
  120.7 3.2 %copy.28 = bf16[2,8,8,64,64]{3,2,4,1,0:T(8,128)(2,1)S(1)} copy(bf16[2,8,8,64,64]{4,3,0,1,2:T(8,128)(2,1)} %bitcast_bitcast_fusion) | data formatting | bytes 2097152 | tf_op jit(solution)/shard_map/reshape | solution.py:46
  124.0 2.0 %reshape.47 = bf16[2,8,512,64]{2,3,1,0:T(8,128)(2,1)} reshape(bf16[2,8,8,64,64]{3,2,4,1,0:T(8,128)(2,1)S(1)} %copy.28) | data formatting | bytes 2097152 | tf_op jit(solution)/shard_map/reshape | solution.py:46
  126.0 4.3 %fusion.25 = bf16[2,512,64]{1,2,0:T(8,128)(2,1)S(1)} fusion(bf16[2,512,512]{2,1,0:T(8,128)(2,1)S(1)} %copy-done, bf16[2,8,512,64]{2,3,1,0:T(8,128)(2,1)} %reshape.47, bf16[8,512,512]{2,1,0:T(8,128)(2,1)} %param.12), kind=kOutput, calls=%fused_computation.17 | convolution fusion | flops 604110848 | bytes 6422528 | tf_op jit(solution)/shard_map/jab,jbc->jac/dot_general | solution.py:53
  130.5 0.2 reshape.56
  130.8 11.5 %all_to_all.42 = bf16[8,2,4096]{2,1,0:T(2,128)(2,1)S(1)} all-to-all(bf16[8,2,4096]{2,1,0:T(2,128)(2,1)S(1)} %reshape.56), channel_id=1, replica_groups=mesh['blk'=32,'sub'=8] {'sub'}, dimensions={0} | all-to-all | bytes 262144 | tf_op jit(solution)/shard_map/all_to_all | solution.py:56
  142.2 0.2 reshape.57
  142.6 0.2 all_to_all.33
  142.9 2.1 %convolution_convert_fusion = bf16[2,64,512]{2,1,0:T(8,128)(2,1)S(1)} fusion(bf16[2,512,512]{2,1,0:T(8,128)(2,1)S(1)} %copy-done.3, bf16[2,64,512]{2,1,0:T(8,128)(2,1)S(1)} %all_to_all.33, bf16[2,512,512]{2,1,0:T(8,128)(2,1)} %param.19, f32[2,512]{1,0:T(2,128)S(1)} %copy-done.4, f32[2,64]{1,0:T(2,128)S(1)} %copy-done.5), kind=kOutput, calls=%fused_computation.14 | convolution fusion | flops 134479872 | bytes 2363904 | tf_op jit(solution)/shard_map/jrm,jkm->jrk/dot_general | solution.py:59
  145.1 0.2 reshape.58
  145.4 11.5 %all_to_all.43 = bf16[8,2,4096]{2,1,0:T(2,128)(2,1)S(1)} all-to-all(bf16[8,2,4096]{2,1,0:T(2,128)(2,1)S(1)} %reshape.58), channel_id=1, replica_groups=mesh['blk'=32,'sub'=8] {'sub'}, dimensions={0} | all-to-all | bytes 262144 | tf_op jit(solution)/shard_map/all_to_all | solution.py:62
  156.8 0.2 reshape.59
  157.2 0.2 all_to_all.37
  157.5 1.1 convolution_bitcast_fusion
  (28 shorter events, 1.8 us)
Async XLA Ops:
  6.5 119.5 %copy-start = (bf16[2,512,512]{2,1,0:T(8,128)(2,1)S(1)}, bf16[2,512,512]{2,1,0:T(8,128)(2,1)}, u32[]{:S(2)}) copy-start(bf16[2,512,512]{2,1,0:T(8,128)(2,1)} %param.17) | copy-start | bytes 3145732
  6.5 57.1 %all-gather.2.cloned.1.call-start = ((), (), s32[]{:S(2)}) async-start(), calls=%async_computation.3 | async-start | bytes 4325376 | tf_op jit(solution)/shard_map/all_gather | solution.py:38
  75.3 1.4 copy-start.1
  130.3 12.5 %copy-start.3 = (bf16[2,512,512]{2,1,0:T(8,128)(2,1)S(1)}, bf16[2,512,512]{2,1,0:T(8,128)(2,1)}, u32[]{:S(2)}) copy-start(bf16[2,512,512]{2,1,0:T(8,128)(2,1)} %param.18) | copy-start | bytes 3145732
  130.3 12.5 %copy-start.4 = (f32[2,512]{1,0:T(2,128)S(1)}, f32[2,512]{1,0:T(2,128)}, u32[]{:S(2)}) copy-start(f32[2,512]{1,0:T(2,128)} %param.21) | copy-start | bytes 12292
  130.3 12.5 %copy-start.5 = (f32[2,64]{1,0:T(2,128)S(1)}, f32[2,64]{1,0:T(2,128)}, u32[]{:S(2)}) copy-start(f32[2,64]{1,0:T(2,128)} %param.20) | copy-start | bytes 1540
  142.9 14.6 %copy-start.2 = (bf16[2,512,512]{2,1,0:T(8,128)(2,1)S(1)}, bf16[2,512,512]{2,1,0:T(8,128)(2,1)}, u32[]{:S(2)}) copy-start(bf16[2,512,512]{2,1,0:T(8,128)(2,1)} %param.16) | copy-start | bytes 3145732
Sparse Core Ops, SparseCore 0:
  9.9 53.7 all-gather.1
